TPU v7x, 128 devices: a whole 4x4x4 slice. The times are simulated.
128 devices in a mesh: space: 32 (over x, z, core), feat: 4 (over y).
Axes of the slice: x: 4, y: 4, z: 4, core: 2. Of those that a mesh axis runs over, the one named last changes fastest.
Arguments:
- inputs: bfloat16 [2, 96, 180, 1024], P(None, 'space', None, 'feat'), may hold values from -15 to 15
- cotangent: bfloat16 [2, 96, 180, 1024], P(None, 'space', None, 'feat'), may hold values from -6 to 6
- spec_w1: float32 [2, 8, 128, 128], P(None, 'feat'), may hold values from -0.375 to 0.375
- spec_b1: float32 [2, 1024], P(None, 'feat'), may hold values from -0.3 to 0.3
- spec_w2: float32 [2, 8, 128, 128], P(None, 'feat'), may hold values from -0.375 to 0.375
- spec_b2: float32 [2, 1024], P(None, 'feat'), may hold values from -0.3 to 0.3
- up_weight: bfloat16 [1024, 4096], P(None, 'feat'), may hold values from -0.1875 to 0.1875
- down_weight: bfloat16 [4096, 1024], P('feat'), may hold values from -0.09375 to 0.09375
Outputs:
- output: bfloat16 [2, 96, 180, 1024], P(None, 'space', None, 'feat')
- grad_input: bfloat16 [2, 96, 180, 1024], P(None, 'space', None, 'feat')
All inputs are finite; a program needn't handle non-finite values.
Results may differ from a plain program's by a relative error of at most 0.0102.
Values may be sent and summed in bfloat16 or wider, within the bound.
No kernel may reach another device: no remote copies, remote signals or barrier semaphores. Data moves between devices by JAX's collectives and lax.ppermute only.
A program may use at most 128 MiB of HBM per device.

v0:
```python
import math
import jax
import jax.numpy as jnp
from jax import lax
from jax.sharding import PartitionSpec as P

EPSILON = 1e-05
SHRINK_LEVEL = 0.1
HIGHEST = lax.Precision.HIGHEST


def longitude_tables(width_lon):
    mode_count = width_lon // 2 + 1
    cell_index = jnp.arange(width_lon, dtype=jnp.int32)[:, None]
    wave_number = jnp.arange(mode_count, dtype=jnp.int32)[None, :]
    phase_angle = (
        2.0 * math.pi / width_lon * (cell_index * wave_number % width_lon).astype(jnp.float32)
    )
    scaling = 1.0 / math.sqrt(width_lon)
    cos_fwd = jnp.cos(phase_angle) * scaling
    sin_fwd = -jnp.sin(phase_angle) * scaling
    doubled = jnp.where((wave_number == 0) | (wave_number * 2 == width_lon), 1.0, 2.0).astype(
        jnp.float32
    )
    return (cos_fwd, sin_fwd, cos_fwd * doubled, sin_fwd * doubled)


def padded_tables(width_lon, multiple):
    tables = longitude_tables(width_lon)
    modes = tables[0].shape[1]
    extra = -modes % multiple
    return tuple((jnp.pad(table, ((0, 0), (0, extra))) for table in tables))


def lat_apply(table, field):
    return jnp.einsum("gh,bhkc->bgkc", table, field, precision=HIGHEST)


def complex_latitude(table_cos, table_sin, real_part, imag_part, inverse):
    if inverse:
        return (
            lat_apply(table_cos, real_part) + lat_apply(table_sin, imag_part),
            lat_apply(table_cos, imag_part) - lat_apply(table_sin, real_part),
        )
    return (
        lat_apply(table_cos, real_part) - lat_apply(table_sin, imag_part),
        lat_apply(table_cos, imag_part) + lat_apply(table_sin, real_part),
    )


def lon_forward(field, table):
    return jnp.einsum("brwc,wk->brkc", field, table, precision=HIGHEST)


def lon_back(spec, table):
    return jnp.einsum("brkc,wk->brwc", spec, table, precision=HIGHEST)


def to_blocks(field, block_size):
    return field.reshape(field.shape[:-1] + (field.shape[-1] // block_size, block_size))


def block_mult(field, weights):
    return jnp.einsum("...nc,nce->...ne", field, weights, precision=HIGHEST)


def block_mult_back(field, weights):
    return jnp.einsum("...ne,nce->...nc", field, weights, precision=HIGHEST)


def block_product(real_part, imag_part, weights):
    return (
        block_mult(real_part, weights[0]) - block_mult(imag_part, weights[1]),
        block_mult(real_part, weights[1]) + block_mult(imag_part, weights[0]),
    )


def block_adjoint(real_part, imag_part, weights):
    return (
        block_mult_back(real_part, weights[0]) + block_mult_back(imag_part, weights[1]),
        block_mult_back(imag_part, weights[0]) - block_mult_back(real_part, weights[1]),
    )


def latitude_tables(length):
    index_row = jnp.arange(length, dtype=jnp.int32)
    phase_angle = (
        2.0
        * math.pi
        / length
        * (index_row[:, None] * index_row[None, :] % length).astype(jnp.float32)
    )
    scaling = 1.0 / math.sqrt(length)
    return (jnp.cos(phase_angle) * scaling, -jnp.sin(phase_angle) * scaling)


def to_columns(real_part, imag_part):
    stacked = jnp.stack([real_part, imag_part])
    moved = lax.all_to_all(stacked, "space", 3, 2, tiled=True)
    return (moved[0], moved[1])


def to_rows(real_part, imag_part):
    stacked = jnp.stack([real_part, imag_part])
    moved = lax.all_to_all(stacked, "space", 2, 3, tiled=True)
    return (moved[0], moved[1])


def enter_spectrum(real_part, imag_part):
    length = real_part.shape[1] * lax.axis_size("space")
    table_cos, table_sin = latitude_tables(length)
    real_part, imag_part = to_columns(real_part, imag_part)
    return complex_latitude(table_cos, table_sin, real_part, imag_part, False)


def leave_spectrum(real_part, imag_part):
    table_cos, table_sin = latitude_tables(real_part.shape[1])
    real_part, imag_part = complex_latitude(table_cos, table_sin, real_part, imag_part, True)
    return to_rows(real_part, imag_part)


def token_sums(first_term, second_term):
    pair = jnp.stack([first_term, second_term])
    count = lax.axis_size("feat")
    bit = 1
    while bit < count:
        pair = pair + lax.ppermute(pair, "feat", [(i, i ^ bit) for i in range(count)])
        bit *= 2
    return (pair[0], pair[1])


def ring_send(block):
    count = lax.axis_size("feat")
    return [block] + [
        lax.ppermute(block, "feat", [(i, (i + shift) % count) for i in range(count)])
        for shift in range(1, count)
    ]


def ring_assemble(parts):
    count = len(parts)
    position = lax.axis_index("feat")
    block = parts[0]
    width = block.shape[-1]
    whole = jnp.zeros(block.shape[:-1] + (width * count,), block.dtype)
    for shift, moved in enumerate(parts):
        source = (position + count - shift) % count
        whole = lax.dynamic_update_slice_in_dim(whole, moved, source * width, axis=block.ndim - 1)
    return whole


def channel_share(term):
    return lax.psum_scatter(
        term.astype(jnp.bfloat16), "feat", scatter_dimension=3, tiled=True
    ).astype(jnp.float32)


def gelu_value(field):
    return 0.5 * field * (1.0 + lax.erf(field * (1.0 / math.sqrt(2.0))))


def gelu_slope(field):
    return 0.5 * (1.0 + lax.erf(field * (1.0 / math.sqrt(2.0)))) + field * jnp.exp(
        -0.5 * field * field
    ) * (1.0 / math.sqrt(2.0 * math.pi))


def spectral_forward(field, spec_w1, spec_b1, spec_w2, spec_b2, cos_fwd, sin_fwd):
    block_size = spec_w1.shape[2]
    spec_real, spec_imag = enter_spectrum(lon_forward(field, cos_fwd), lon_forward(field, sin_fwd))
    spec_shape = spec_real.shape
    bias_one = to_blocks(spec_b1, block_size)
    bias_two = to_blocks(spec_b2, block_size)
    first_real, first_imag = block_product(
        to_blocks(spec_real, block_size), to_blocks(spec_imag, block_size), spec_w1
    )
    first_real = jax.nn.relu(first_real + bias_one[0])
    first_imag = jax.nn.relu(first_imag + bias_one[1])
    second_real, second_imag = block_product(first_real, first_imag, spec_w2)
    second_real = second_real + bias_two[0]
    second_imag = second_imag + bias_two[1]
    shrunk_real = (second_real - jnp.clip(second_real, -SHRINK_LEVEL, SHRINK_LEVEL)).reshape(
        spec_shape
    )
    shrunk_imag = (second_imag - jnp.clip(second_imag, -SHRINK_LEVEL, SHRINK_LEVEL)).reshape(
        spec_shape
    )
    back = complex_latitude_inverse(shrunk_real, shrunk_imag)
    return (back, (first_real, first_imag, second_real, second_imag))


def complex_latitude_inverse(real_part, imag_part):
    table_cos, table_sin = latitude_tables(real_part.shape[1])
    return complex_latitude(table_cos, table_sin, real_part, imag_part, True)


def spectral_leave(back, cos_inv, sin_inv):
    back_real, back_imag = to_rows(*back)
    return lon_back(back_real, cos_inv) + lon_back(back_imag, sin_inv)


def spectral_backward(grad_field, saved, spec_w1, spec_w2, cos_fwd, sin_fwd, cos_inv, sin_inv):
    block_size = spec_w1.shape[2]
    first_real, first_imag, second_real, second_imag = saved
    grad_real, grad_imag = enter_spectrum(
        lon_forward(grad_field, cos_inv), lon_forward(grad_field, sin_inv)
    )
    spec_shape = grad_real.shape
    grad_real = jnp.where(
        jnp.abs(second_real) > SHRINK_LEVEL, to_blocks(grad_real, block_size), 0.0
    )
    grad_imag = jnp.where(
        jnp.abs(second_imag) > SHRINK_LEVEL, to_blocks(grad_imag, block_size), 0.0
    )
    first_grad_real, first_grad_imag = block_adjoint(grad_real, grad_imag, spec_w2)
    first_grad_real = jnp.where(first_real > 0.0, first_grad_real, 0.0)
    first_grad_imag = jnp.where(first_imag > 0.0, first_grad_imag, 0.0)
    spec_grad_real, spec_grad_imag = block_adjoint(first_grad_real, first_grad_imag, spec_w1)
    rows_real, rows_imag = leave_spectrum(
        spec_grad_real.reshape(spec_shape), spec_grad_imag.reshape(spec_shape)
    )
    return lon_back(rows_real, cos_fwd) + lon_back(rows_imag, sin_fwd)


def per_device(inputs, cotangent, spec_w1, spec_b1, spec_w2, spec_b2, up_weight, down_weight):
    full_width = up_weight.shape[0]
    block_size = spec_w1.shape[2]
    cos_fwd, sin_fwd, cos_inv, sin_inv = padded_tables(inputs.shape[2], lax.axis_size("space"))
    values = inputs.astype(jnp.float32)
    cotangent_parts = ring_send(cotangent)
    first_sum, second_sum = token_sums(jnp.sum(values, axis=-1), jnp.sum(values * values, axis=-1))
    mean_one = first_sum[..., None] / full_width
    rstd_one = lax.rsqrt(second_sum[..., None] / full_width - mean_one * mean_one + EPSILON)
    normed = (values - mean_one) * rstd_one
    block_count = spec_w1.shape[1]
    shrunk_parts, saved_parts = ([], [])
    for block in range(block_count):
        channels = slice(block * block_size, (block + 1) * block_size)
        shrunk, saved = spectral_forward(
            normed[..., channels],
            spec_w1[:, block : block + 1],
            spec_b1[:, channels],
            spec_w2[:, block : block + 1],
            spec_b2[:, channels],
            cos_fwd,
            sin_fwd,
        )
        shrunk_parts.append(shrunk)
        saved_parts.append(saved)
    shrunk_parts[-1], cotangent_parts = lax.optimization_barrier(
        (shrunk_parts[-1], cotangent_parts)
    )
    whole_cotangent = ring_assemble(cotangent_parts)
    filtered = jnp.concatenate(
        [spectral_leave(shrunk, cos_inv, sin_inv) for shrunk in shrunk_parts], axis=-1
    )
    residual = (filtered + normed + values).astype(jnp.bfloat16)
    residual_vals = residual.astype(jnp.float32)
    whole_residual = lax.all_gather(residual, "feat", axis=3, tiled=True)
    whole_vals = whole_residual.astype(jnp.float32)
    mean_two = jnp.sum(whole_vals, axis=-1, keepdims=True) / full_width
    square_two = jnp.sum(whole_vals * whole_vals, axis=-1, keepdims=True) / full_width
    rstd_two = lax.rsqrt(square_two - mean_two * mean_two + EPSILON)
    vhat = (whole_vals - mean_two) * rstd_two
    hidden = jnp.einsum(
        "brwd,dh->brwh", vhat.astype(jnp.bfloat16), up_weight, preferred_element_type=jnp.float32
    )
    activated = gelu_value(hidden).astype(jnp.bfloat16)
    mixed_term = jnp.einsum(
        "brwh,hd->brwd", activated, down_weight, preferred_element_type=jnp.float32
    )
    output = (residual_vals + channel_share(mixed_term)).astype(jnp.bfloat16)
    grad_act = jnp.einsum(
        "brwd,hd->brwh", whole_cotangent, down_weight, preferred_element_type=jnp.float32
    )
    grad_hidden = (grad_act * gelu_slope(hidden)).astype(jnp.bfloat16)
    grad_term = jnp.einsum(
        "brwh,dh->brwd", grad_hidden, up_weight, preferred_element_type=jnp.float32
    )
    total_one, total_two = token_sums(
        jnp.sum(grad_term, axis=-1), jnp.sum(grad_term * vhat, axis=-1)
    )
    grad_vhat = channel_share(grad_term)
    own_hat = (residual_vals - mean_two) * rstd_two
    grad_residual = cotangent.astype(jnp.float32) + rstd_two * (
        grad_vhat
        - total_one[..., None] / full_width
        - own_hat * (total_two[..., None] / full_width)
    )
    grad_filter = jnp.concatenate(
        [
            spectral_backward(
                grad_residual[..., block * block_size : (block + 1) * block_size],
                saved_parts[block],
                spec_w1[:, block : block + 1],
                spec_w2[:, block : block + 1],
                cos_fwd,
                sin_fwd,
                cos_inv,
                sin_inv,
            )
            for block in range(block_count)
        ],
        axis=-1,
    )
    grad_normed = grad_residual + grad_filter
    norm_one, norm_two = token_sums(
        jnp.sum(grad_normed, axis=-1), jnp.sum(grad_normed * normed, axis=-1)
    )
    grad_input = grad_residual + rstd_one * (
        grad_normed - norm_one[..., None] / full_width - normed * (norm_two[..., None] / full_width)
    )
    return (output, grad_input.astype(jnp.bfloat16))


def solution(mesh):
    return jax.shard_map(
        per_device,
        mesh=mesh,
        in_specs=(
            P(None, "space", None, "feat"),
            P(None, "space", None, "feat"),
            P(None, "feat", None, None),
            P(None, "feat"),
            P(None, "feat", None, None),
            P(None, "feat"),
            P(None, "feat"),
            P("feat", None),
        ),
        out_specs=(P(None, "space", None, "feat"), P(None, "space", None, "feat")),
        check_vma=False,
    )
```

profile of v0, /device:TPU:0, one launch (start us, length us, event | category | flops | bytes accessed | tf_op | source)
XLA Modules:
  0.0 356.5 jit_solution(820768273294857177)
XLA Ops:
  7.2 3.2 collective-permute-start.4
  17.2 17.8 %collective-permute-done = f32[2,2,3,180]{3,2,1,0:T(4,128)S(1)} collective-permute-done((f32[2,2,3,180]{3,2,1,0:T(4,128)S(1)}, f32[2,2,3,180]{3,2,1,0:T(4,128)S(1)}, u32[]{:S(2)}, u32[]{:S(2)}) %collective-permute-start) | collective-permute-done | bytes 8672 | tf_op jit(solution)/shard_map/ppermute | solution.py:127
  35.0 3.1 collective-permute-start.1
  44.0 8.3 %all-to-all-start = ((f32[2,2,3,96,128]{4,1,2,0,3:T(2,128)}), f32[2,2,3,96,128]{4,1,2,0,3:T(2,128)}, u32[]{:S(2)}, u32[]{:S(2)}) async-start(f32[2,2,3,96,128]{4,1,2,0,3:T(2,128)} %copy.147), calls=%async_computation | async-start | bytes 1179648 | tf_op jit(solution)/shard_map/all_to_all | solution.py:99
  55.2 8.9 %all-to-all-done = f32[2,2,3,96,128]{4,1,2,0,3:T(2,128)} async-done(((f32[2,2,3,96,128]{4,1,2,0,3:T(2,128)}), f32[2,2,3,96,128]{4,1,2,0,3:T(2,128)}, u32[]{:S(2)}, u32[]{:S(2)}) %all-to-all-start) | async-done | bytes 589856 | tf_op jit(solution)/shard_map/all_to_all | solution.py:99
  64.1 4.6 %all-to-all-start.2 = ((f32[2,2,3,96,128]{4,1,2,0,3:T(2,128)}), f32[2,2,3,96,128]{4,1,2,0,3:T(2,128)S(1)}, u32[]{:S(2)}, u32[]{:S(2)}) async-start(f32[2,2,3,96,128]{4,1,2,0,3:T(2,128)} %copy.161), calls=%async_computation.2 | async-start | bytes 1179648 | tf_op jit(solution)/shard_map/all_to_all | solution.py:99
  92.2 4.6 %all-to-all-start.1 = ((f32[2,2,96,3,128]{4,1,3,0,2:T(2,128)}), f32[2,2,96,3,128]{4,1,3,0,2:T(2,128)}, u32[]{:S(2)}, u32[]{:S(2)}) async-start(f32[2,2,96,3,128]{4,1,3,0,2:T(2,128)} %copy.155), calls=%async_computation.1 | async-start | bytes 1179648 | tf_op jit(solution)/shard_map/all_to_all | solution.py:105
  103.0 5.5 %all-to-all-done.1 = f32[2,2,96,3,128]{4,1,3,0,2:T(2,128)} async-done(((f32[2,2,96,3,128]{4,1,3,0,2:T(2,128)}), f32[2,2,96,3,128]{4,1,3,0,2:T(2,128)}, u32[]{:S(2)}, u32[]{:S(2)}) %all-to-all-start.1) | async-done | bytes 589856 | tf_op jit(solution)/shard_map/all_to_all | solution.py:105
  108.5 4.1 %all-to-all-start.3 = ((f32[2,2,96,3,128]{4,1,3,0,2:T(2,128)}), f32[2,2,96,3,128]{4,1,3,0,2:T(2,128)S(1)}, u32[]{:S(2)}, u32[]{:S(2)}) async-start(f32[2,2,96,3,128]{4,1,3,0,2:T(2,128)} %copy.169), calls=%async_computation.3 | async-start | bytes 1179648 | tf_op jit(solution)/shard_map/all_to_all | solution.py:105
  115.6 8.9 %all-to-all-done.3 = f32[2,2,96,3,128]{4,1,3,0,2:T(2,128)S(1)} async-done(((f32[2,2,96,3,128]{4,1,3,0,2:T(2,128)}), f32[2,2,96,3,128]{4,1,3,0,2:T(2,128)S(1)}, u32[]{:S(2)}, u32[]{:S(2)}) %all-to-all-start.3) | async-done | bytes 589856 | tf_op jit(solution)/shard_map/all_to_all | solution.py:105
  137.9 26.5 %all-gather.2.cloned.1.call-done = bf16[2,3,180,1024]{3,2,1,0:T(8,128)(2,1)} async-done(((bf16[2,3,180,256]{3,2,1,0:T(8,128)(2,1)}), bf16[2,3,180,1024]{3,2,1,0:T(8,128)(2,1)}) %all-gather.2.cloned.1.call-update) | async-done | bytes 2211856 | tf_op jit(solution)/shard_map/all_gather | solution.py:259
  167.1 5.0 %fusion.14 = f32[2,3,180,1024]{3,2,1,0:T(8,128)} fusion(bf16[2,3,180,1024]{3,2,1,0:T(8,128)(2,1)S(1)} %copy-done.32, f32[2,3,180]{2,1,0:T(4,128)S(1)} %get-tuple-element.54, f32[2,3,180]{2,1,0:T(4,128)S(1)} %get-tuple-element.53, bf16[1024,1024]{1,0:T(8,128)(2,1)S(1)} %copy-done), kind=kOutput, calls=%fused_computation.19 | convolution fusion | flops 2269347840 | bytes 8741312 | tf_op jit(solution)/shard_map/brwd,dh->brwh/dot_general | solution.py:265
  172.1 11.0 %fusion.552 = (f32[2,3,180]{2,1,0:T(4,128)S(1)}, f32[2,3,180]{2,1,0:T(4,128)S(1)}, bf16[2,3,180,1024]{3,2,1,0:T(8,128)(2,1)}) fusion(f32[2,3,180]{2,1,0:T(4,128)S(1)} %get-tuple-element.54, f32[2,3,180]{2,1,0:T(4,128)S(1)} %get-tuple-element.53, bf16[2,3,180,1024]{3,2,1,0:T(8,128)(2,1)} %all-gather.2.cloned.1.call-done, ...), kind=kOutput, calls=%fused_computation.644 | convolution fusion | flops 4548646912 | bytes 15270784 | tf_op jit(solution)/shard_map/brwh,dh->brwd/dot_general | solution.py:277
  184.7 6.2 %fusion.27 = bf16[2,3,180,1024]{3,2,1,0:T(8,128)(2,1)} fusion(bf16[1024,1024]{1,0:T(8,128)(2,1)S(1)} %copy-done.45, f32[2,3,180,1024]{3,2,1,0:T(8,128)} %fusion.14), kind=kOutput, calls=%fused_computation.35 | convolution fusion | flops 2271559680 | bytes 8732672 | tf_op jit(solution)/shard_map/brwh,hd->brwd/dot_general | solution.py:269
  200.4 15.2 %reduce-scatter.5.cloned.1.call-done = bf16[2,3,180,256]{3,2,1,0:T(8,128)(2,1)} async-done(((bf16[2,3,180,1024]{3,2,1,0:T(8,128)(2,1)}), bf16[2,3,180,256]{3,2,1,0:T(8,128)(2,1)}) %reduce-scatter.5.cloned.1.call-update) | async-done | bytes 552976 | tf_op jit(solution)/shard_map/reduce_scatter | solution.py:153
  215.6 33.3 %reduce-scatter.3.cloned.1.call-done = bf16[2,3,180,256]{3,2,1,0:T(8,128)(2,1)} async-done(((bf16[2,3,180,1024]{3,2,1,0:T(8,128)(2,1)}), bf16[2,3,180,256]{3,2,1,0:T(8,128)(2,1)}) %reduce-scatter.3.cloned.1.call-update) | async-done | bytes 552976 | tf_op jit(solution)/shard_map/reduce_scatter | solution.py:153
  253.7 7.6 %all-to-all-start.6 = ((f32[2,2,3,96,128]{4,1,2,0,3:T(2,128)}), f32[2,2,3,96,128]{4,1,2,0,3:T(2,128)S(1)}, u32[]{:S(2)}, u32[]{:S(2)}) async-start(f32[2,2,3,96,128]{4,1,2,0,3:T(2,128)} %copy.194), calls=%async_computation.8 | async-start | bytes 1179648 | tf_op jit(solution)/shard_map/all_to_all | solution.py:99
  263.7 9.5 %all-to-all-done.6 = f32[2,2,3,96,128]{4,1,2,0,3:T(2,128)S(1)} async-done(((f32[2,2,3,96,128]{4,1,2,0,3:T(2,128)}), f32[2,2,3,96,128]{4,1,2,0,3:T(2,128)S(1)}, u32[]{:S(2)}, u32[]{:S(2)}) %all-to-all-start.6) | async-done | bytes 589856 | tf_op jit(solution)/shard_map/all_to_all | solution.py:99
  273.2 4.1 %all-to-all-start.4 = ((f32[2,2,3,96,128]{4,1,2,0,3:T(2,128)}), f32[2,2,3,96,128]{4,1,2,0,3:T(2,128)S(1)}, u32[]{:S(2)}, u32[]{:S(2)}) async-start(f32[2,2,3,96,128]{4,1,2,0,3:T(2,128)} %copy.180), calls=%async_computation.6 | async-start | bytes 1179648 | tf_op jit(solution)/shard_map/all_to_all | solution.py:99
  278.6 10.6 %all-to-all-done.4 = f32[2,2,3,96,128]{4,1,2,0,3:T(2,128)S(1)} async-done(((f32[2,2,3,96,128]{4,1,2,0,3:T(2,128)}), f32[2,2,3,96,128]{4,1,2,0,3:T(2,128)S(1)}, u32[]{:S(2)}, u32[]{:S(2)}) %all-to-all-start.4) | async-done | bytes 589856 | tf_op jit(solution)/shard_map/all_to_all | solution.py:99
  299.7 4.9 %all-to-all-start.5 = ((f32[2,2,96,3,128]{4,1,3,0,2:T(2,128)}), f32[2,2,96,3,128]{4,1,3,0,2:T(2,128)}, u32[]{:S(2)}, u32[]{:S(2)}) async-start(f32[2,2,96,3,128]{4,1,3,0,2:T(2,128)} %copy.188), calls=%async_computation.7 | async-start | bytes 1179648 | tf_op jit(solution)/shard_map/all_to_all | solution.py:105
  316.4 6.9 %all-to-all-start.7 = ((f32[2,2,96,3,128]{4,1,3,0,2:T(2,128)}), f32[2,2,96,3,128]{4,1,3,0,2:T(2,128)S(1)}, u32[]{:S(2)}, u32[]{:S(2)}) async-start(f32[2,2,96,3,128]{4,1,3,0,2:T(2,128)} %copy.202), calls=%async_computation.9 | async-start | bytes 1179648 | tf_op jit(solution)/shard_map/all_to_all | solution.py:105
  325.6 9.5 %all-to-all-done.7 = f32[2,2,96,3,128]{4,1,3,0,2:T(2,128)S(1)} async-done(((f32[2,2,96,3,128]{4,1,3,0,2:T(2,128)}), f32[2,2,96,3,128]{4,1,3,0,2:T(2,128)S(1)}, u32[]{:S(2)}, u32[]{:S(2)}) %all-to-all-start.7) | async-done | bytes 589856 | tf_op jit(solution)/shard_map/all_to_all | solution.py:105
  338.8 3.5 collective-permute-done.7
  (276 shorter events, 117.6 us)
Async XLA Ops:
  7.2 159.9 %copy-start = (bf16[1024,1024]{1,0:T(8,128)(2,1)S(1)}, bf16[1024,1024]{1,0:T(8,128)(2,1)}, u32[]{:S(2)}) copy-start(bf16[1024,1024]{1,0:T(8,128)(2,1)} %param.14) | copy-start | bytes 6291460
  7.2 94.4 %collective-permute-start.4 = (bf16[2,3,180,256]{3,0,2,1:T(2,128)(2,1)}, bf16[2,3,180,256]{3,0,2,1:T(2,128)(2,1)}, u32[]{:S(2)}, u32[]{:S(2)}) collective-permute-start(bf16[2,3,180,256]{3,0,2,1:T(2,128)(2,1)} %param.9), channel_id=1, source_target_pairs={{0,3},{1,0},{2,1},{3,2},{4,7},{5,4},{6,5},{7,6},{8,11},{9,8},{10,9... | collective-permute-start | bytes 1658888 | tf_op jit(solution)/shard_map/ppermute | solution.py:135
  10.3 91.3 %collective-permute-start.3 = (bf16[2,3,180,256]{3,0,2,1:T(2,128)(2,1)}, bf16[2,3,180,256]{3,0,2,1:T(2,128)(2,1)}, u32[]{:S(2)}, u32[]{:S(2)}) collective-permute-start(bf16[2,3,180,256]{3,0,2,1:T(2,128)(2,1)} %param.9), channel_id=1, source_target_pairs={{0,2},{1,3},{2,0},{3,1},{4,6},{5,7},{6,4},{7,5},{8,10},{9,11},{10,... | collective-permute-start | bytes 1658888 | tf_op jit(solution)/shard_map/ppermute | solution.py:135
  11.0 90.7 %collective-permute-start.2 = (bf16[2,3,180,256]{3,0,2,1:T(2,128)(2,1)}, bf16[2,3,180,256]{3,0,2,1:T(2,128)(2,1)}, u32[]{:S(2)}, u32[]{:S(2)}) collective-permute-start(bf16[2,3,180,256]{3,0,2,1:T(2,128)(2,1)} %param.9), channel_id=1, source_target_pairs={{0,1},{1,2},{2,3},{3,0},{4,5},{5,6},{6,7},{7,4},{8,9},{9,10},{10,1... | collective-permute-start | bytes 1658888 | tf_op jit(solution)/shard_map/ppermute | solution.py:135
  13.5 21.4 %collective-permute-start = (f32[2,2,3,180]{3,2,1,0:T(4,128)S(1)}, f32[2,2,3,180]{3,2,1,0:T(4,128)S(1)}, u32[]{:S(2)}, u32[]{:S(2)}) collective-permute-start(f32[2,2,3,180]{3,2,1,0:T(4,128)S(1)} %pad_maximum_fusion.8), channel_id=1, source_target_pairs={{0,1},{1,0},{2,3},{3,2},{4,5},{5,4},{6,7},{7,6},{8,9},{9,8},{10,11... | collective-permute-start | bytes 25928 | tf_op jit(solution)/shard_map/ppermute | solution.py:127
  35.0 5.3 %collective-permute-start.1 = (f32[2,2,3,180]{3,2,1,0:T(4,128)S(1)}, f32[2,2,3,180]{3,2,1,0:T(4,128)S(1)}, u32[]{:S(2)}, u32[]{:S(2)}) collective-permute-start(f32[2,2,3,180]{3,2,1,0:T(4,128)S(1)} %fusion.551), channel_id=1, source_target_pairs={{0,2},{1,3},{2,0},{3,1},{4,6},{5,7},{6,4},{7,5},{8,10},{9,11},{10,... | collective-permute-start | bytes 25928 | tf_op jit(solution)/shard_map/ppermute | solution.py:127
  44.0 20.1 %all-to-all-start = ((f32[2,2,3,96,128]{4,1,2,0,3:T(2,128)}), f32[2,2,3,96,128]{4,1,2,0,3:T(2,128)}, u32[]{:S(2)}, u32[]{:S(2)}) async-start(f32[2,2,3,96,128]{4,1,2,0,3:T(2,128)} %copy.147), calls=%async_computation | async-start | bytes 1179648 | tf_op jit(solution)/shard_map/all_to_all | solution.py:99
  64.1 16.0 %all-to-all-start.2 = ((f32[2,2,3,96,128]{4,1,2,0,3:T(2,128)}), f32[2,2,3,96,128]{4,1,2,0,3:T(2,128)S(1)}, u32[]{:S(2)}, u32[]{:S(2)}) async-start(f32[2,2,3,96,128]{4,1,2,0,3:T(2,128)} %copy.161), calls=%async_computation.2 | async-start | bytes 1179648 | tf_op jit(solution)/shard_map/all_to_all | solution.py:99
  92.2 16.4 %all-to-all-start.1 = ((f32[2,2,96,3,128]{4,1,3,0,2:T(2,128)}), f32[2,2,96,3,128]{4,1,3,0,2:T(2,128)}, u32[]{:S(2)}, u32[]{:S(2)}) async-start(f32[2,2,96,3,128]{4,1,3,0,2:T(2,128)} %copy.155), calls=%async_computation.1 | async-start | bytes 1179648 | tf_op jit(solution)/shard_map/all_to_all | solution.py:105
  108.5 16.0 %all-to-all-start.3 = ((f32[2,2,96,3,128]{4,1,3,0,2:T(2,128)}), f32[2,2,96,3,128]{4,1,3,0,2:T(2,128)S(1)}, u32[]{:S(2)}, u32[]{:S(2)}) async-start(f32[2,2,96,3,128]{4,1,3,0,2:T(2,128)} %copy.169), calls=%async_computation.3 | async-start | bytes 1179648 | tf_op jit(solution)/shard_map/all_to_all | solution.py:105
  112.7 51.8 %all-gather.2.cloned.1.call-start = ((), (), s32[]{:S(2)}) async-start(), calls=%async_computation.10 | async-start | bytes 2826240 | tf_op jit(solution)/shard_map/all_gather | solution.py:259
  129.2 86.4 %reduce-scatter.5.cloned.1.call-start = ((), (), s32[]{:S(2)}) async-start(), calls=%async_computation.12 | async-start | bytes 2826240 | tf_op jit(solution)/shard_map/reduce_scatter | solution.py:153
  183.1 65.8 %reduce-scatter.3.cloned.1.call-start = ((), (), s32[]{:S(2)}) async-start(), calls=%async_computation.11 | async-start | bytes 2826240 | tf_op jit(solution)/shard_map/reduce_scatter | solution.py:153
  190.9 58.1 %copy-start.4 = (bf16[2,3,180,256]{3,2,1,0:T(8,128)(2,1)S(1)}, bf16[2,3,180,256]{3,2,1,0:T(8,128)(2,1)}, u32[]{:S(2)}) copy-start(bf16[2,3,180,256]{3,2,1,0:T(8,128)(2,1)} %fusion.102) | copy-start | bytes 1658884
  190.9 58.1 %copy-start.34 = (bf16[2,3,180,256]{3,0,2,1:T(2,128)(2,1)S(1)}, bf16[2,3,180,256]{3,0,2,1:T(2,128)(2,1)}, u32[]{:S(2)}) copy-start(bf16[2,3,180,256]{3,0,2,1:T(2,128)(2,1)} %param.9) | copy-start | bytes 1658884
  190.9 60.6 %copy-start.30 = (f32[180,91]{1,0:T(8,128)S(1)}, f32[180,91]{1,0:T(8,128)}, u32[]{:S(2)}) copy-start(f32[180,91]{1,0:T(8,128)} %copy-done.29) | copy-start | bytes 196564
  190.9 3.8 %collective-permute-start.5 = (f32[2,2,3,180]{3,2,1,0:T(4,128)S(1)}, f32[2,2,3,180]{3,2,1,0:T(4,128)S(1)}, u32[]{:S(2)}, u32[]{:S(2)}) collective-permute-start(f32[2,2,3,180]{3,2,1,0:T(4,128)S(1)} %pad_maximum_fusion.9), channel_id=1, source_target_pairs={{0,1},{1,0},{2,3},{3,2},{4,5},{5,4},{6,7},{7,6},{8,9},{9,8},{10,11... | collective-permute-start | bytes 25928 | tf_op jit(solution)/shard_map/ppermute | solution.py:127
  194.7 5.6 %collective-permute-start.6 = (f32[2,2,3,180]{3,2,1,0:T(4,128)S(1)}, f32[2,2,3,180]{3,2,1,0:T(4,128)S(1)}, u32[]{:S(2)}, u32[]{:S(2)}) collective-permute-start(f32[2,2,3,180]{3,2,1,0:T(4,128)S(1)} %fusion.550), channel_id=1, source_target_pairs={{0,2},{1,3},{2,0},{3,1},{4,6},{5,7},{6,4},{7,5},{8,10},{9,11},{10,... | collective-permute-start | bytes 25928 | tf_op jit(solution)/shard_map/ppermute | solution.py:127
  253.7 19.5 %all-to-all-start.6 = ((f32[2,2,3,96,128]{4,1,2,0,3:T(2,128)}), f32[2,2,3,96,128]{4,1,2,0,3:T(2,128)S(1)}, u32[]{:S(2)}, u32[]{:S(2)}) async-start(f32[2,2,3,96,128]{4,1,2,0,3:T(2,128)} %copy.194), calls=%async_computation.8 | async-start | bytes 1179648 | tf_op jit(solution)/shard_map/all_to_all | solution.py:99
  273.2 15.9 %all-to-all-start.4 = ((f32[2,2,3,96,128]{4,1,2,0,3:T(2,128)}), f32[2,2,3,96,128]{4,1,2,0,3:T(2,128)S(1)}, u32[]{:S(2)}, u32[]{:S(2)}) async-start(f32[2,2,3,96,128]{4,1,2,0,3:T(2,128)} %copy.180), calls=%async_computation.6 | async-start | bytes 1179648 | tf_op jit(solution)/shard_map/all_to_all | solution.py:99
  299.7 16.7 %all-to-all-start.5 = ((f32[2,2,96,3,128]{4,1,3,0,2:T(2,128)}), f32[2,2,96,3,128]{4,1,3,0,2:T(2,128)}, u32[]{:S(2)}, u32[]{:S(2)}) async-start(f32[2,2,96,3,128]{4,1,3,0,2:T(2,128)} %copy.188), calls=%async_computation.7 | async-start | bytes 1179648 | tf_op jit(solution)/shard_map/all_to_all | solution.py:105
  316.4 18.8 %all-to-all-start.7 = ((f32[2,2,96,3,128]{4,1,3,0,2:T(2,128)}), f32[2,2,96,3,128]{4,1,3,0,2:T(2,128)S(1)}, u32[]{:S(2)}, u32[]{:S(2)}) async-start(f32[2,2,96,3,128]{4,1,3,0,2:T(2,128)} %copy.202), calls=%async_computation.9 | async-start | bytes 1179648 | tf_op jit(solution)/shard_map/all_to_all | solution.py:105
  338.5 3.8 %collective-permute-start.7 = (f32[2,2,3,180]{3,2,1,0:T(4,128)S(1)}, f32[2,2,3,180]{3,2,1,0:T(4,128)S(1)}, u32[]{:S(2)}, u32[]{:S(2)}) collective-permute-start(f32[2,2,3,180]{3,2,1,0:T(4,128)S(1)} %pad_maximum_fusion.10), channel_id=1, source_target_pairs={{0,1},{1,0},{2,3},{3,2},{4,5},{5,4},{6,7},{7,6},{8,9},{9,8},{10,11... | collective-permute-start | bytes 25928 | tf_op jit(solution)/shard_map/ppermute | solution.py:127
  342.3 5.3 %collective-permute-start.8 = (f32[2,2,3,180]{3,2,1,0:T(4,128)S(1)}, f32[2,2,3,180]{3,2,1,0:T(4,128)S(1)}, u32[]{:S(2)}, u32[]{:S(2)}) collective-permute-start(f32[2,2,3,180]{3,2,1,0:T(4,128)S(1)} %fusion.549), channel_id=1, source_target_pairs={{0,2},{1,3},{2,0},{3,1},{4,6},{5,7},{6,4},{7,5},{8,10},{9,11},{10,... | collective-permute-start | bytes 25928 | tf_op jit(solution)/shard_map/ppermute | solution.py:127
  (42 other events, 226.8 us)
Sparse Core Ops, SparseCore 0:
  129.3 35.1 all-gather.1
  183.2 32.3 reduce-scatter.4
  218.2 30.7 reduce-scatter.2
where the time goes:
time: 363 us; the launch traced here: 356 us
  waiting for transfers between devices  163 us (45%)
  matrix products  68.6 us (19%)
  starting transfers between devices  61 us (17%)
  local copies, waits for them, and re-layouts  35.2 us (10%)
  between operations  15.7 us (4%)
  other arithmetic  12.5 us (3%)
    reduce_scatter x2, waiting for transfers between devices, channel_share(): lax.psum_scatter(term.astype(jnp.bfloat16), 'feat', scatter_dimension=3,...  48.5 us
    all_to_all x4, waiting for transfers between devices, to_columns(): moved = lax.all_to_all(stacked, 'space', 3, 2, tiled=True)  32 us
    ppermute x6, waiting for transfers between devices, token_sums(): lax.ppermute(pair, 'feat', [(i, i ^ bit) for i in range(count)])  31.4 us
    all_gather x1, waiting for transfers between devices, per_device(): whole_residual = lax.all_gather(residual, 'feat', axis=3, tiled=True)  26.5 us
    all_to_all x4, waiting for transfers between devices, to_rows(): moved = lax.all_to_all(stacked, 'space', 2, 3, tiled=True)  24.9 us
    all_to_all x4, starting transfers between devices, to_columns(): moved = lax.all_to_all(stacked, 'space', 3, 2, tiled=True)  24.7 us
    dot_general x32, matrix products, lat_apply(): return jnp.einsum('gh,bhkc->bgkc', table, field, precision=HIGHEST)  20.6 us
    all_to_all x4, starting transfers between devices, to_rows(): moved = lax.all_to_all(stacked, 'space', 2, 3, tiled=True)  20.6 us
  transfers between devices with their start and end apart: 20, of which 17 were waited for; matrix products, arithmetic and copies ran while one was open for 20% of the time, Pallas kernels for 0%

commit v1 on v0

--- a/solution.py
+++ b/solution.py
@@ -256,7 +256,9 @@
     )
     residual = (filtered + normed + values).astype(jnp.bfloat16)
     residual_vals = residual.astype(jnp.float32)
-    whole_residual = lax.all_gather(residual, "feat", axis=3, tiled=True)
+    whole_residual = jnp.concatenate(
+        lax.all_to_all(jnp.stack([residual] * lax.axis_size("feat")), "feat", 0, 0), axis=3
+    )
     whole_vals = whole_residual.astype(jnp.float32)
     mean_two = jnp.sum(whole_vals, axis=-1, keepdims=True) / full_width
     square_two = jnp.sum(whole_vals * whole_vals, axis=-1, keepdims=True) / full_width

time: 363 us -> 379 us (1.044)
  local copies, waits for them, and re-layouts: 35.2 us -> 51 us
  waiting for transfers between devices: 163 us -> 153 us
  other arithmetic: 12.5 us -> 17.7 us
    all_gather x1 -> x0, waiting for transfers between devices: 26.5 us -> none  [per_device(): whole_residual = lax.all_gather(residual, 'feat', axis=3, tiled=True)]
    all_to_all x0 -> x1, waiting for transfers between devices: none -> 19.9 us  [per_device(): lax.all_to_all(jnp.stack([residual] * lax.axis_size('feat')), 'feat', 0, 0)]
    convert_element_type x0 -> x3, local copies, waits for them, and re-layouts: none -> 11.1 us  [the longest x2 10.7 us: per_device(): whole_vals = whole_residual.astype(jnp.float32)]
    reduce_scatter x2, waiting for transfers between devices: 48.5 us -> 43 us  [channel_share(): lax.psum_scatter(term.astype(jnp.bfloat16), 'feat', scatter_dimension=3,...]
    all_to_all x0 -> x1, starting transfers between devices: none -> 5.32 us  [per_device(): lax.all_to_all(jnp.stack([residual] * lax.axis_size('feat')), 'feat', 0, 0)]
  transfers between devices with their start and end apart: 20 -> 20, of which waited for: 17 -> 17; matrix products, arithmetic and copies ran while one was open for 20% -> 19% of each run, Pallas kernels for 0% -> 0%
where the time goes in v1:
time: 379 us; the launch traced here: 372 us
  waiting for transfers between devices  153 us (40%)
  matrix products  71.1 us (19%)
  starting transfers between devices  64 us (17%)
  local copies, waits for them, and re-layouts  51 us (13%)
  other arithmetic  17.7 us (5%)
  between operations  16.1 us (4%)
    reduce_scatter x2, waiting for transfers between devices, channel_share(): lax.psum_scatter(term.astype(jnp.bfloat16), 'feat', scatter_dimension=3,...  43 us
    ppermute x6, waiting for transfers between devices, token_sums(): lax.ppermute(pair, 'feat', [(i, i ^ bit) for i in range(count)])  33.6 us
    all_to_all x4, waiting for transfers between devices, to_columns(): moved = lax.all_to_all(stacked, 'space', 3, 2, tiled=True)  31.3 us
    all_to_all x4, waiting for transfers between devices, to_rows(): moved = lax.all_to_all(stacked, 'space', 2, 3, tiled=True)  24.9 us
    all_to_all x4, starting transfers between devices, to_columns(): moved = lax.all_to_all(stacked, 'space', 3, 2, tiled=True)  24.5 us
    all_to_all x4, starting transfers between devices, to_rows(): moved = lax.all_to_all(stacked, 'space', 2, 3, tiled=True)  20.7 us
    dot_general x32, matrix products, lat_apply(): return jnp.einsum('gh,bhkc->bgkc', table, field, precision=HIGHEST)  20.6 us
    all_to_all x1, waiting for transfers between devices, per_device(): lax.all_to_all(jnp.stack([residual] * lax.axis_size('feat')), 'feat', 0, 0)  19.9 us
  transfers between devices with their start and end apart: 20, of which 17 were waited for; matrix products, arithmetic and copies ran while one was open for 19% of the time, Pallas kernels for 0%

profile of v1, /device:TPU:0, one launch (start us, length us, event | category | flops | bytes accessed | tf_op | source)
XLA Modules:
  0.0 372.4 jit_solution(5834565305347689990)
XLA Ops:
  17.2 17.7 %collective-permute-done = f32[2,2,3,180]{3,1,2,0:T(2,128)S(1)} collective-permute-done((f32[2,2,3,180]{3,1,2,0:T(2,128)S(1)}, f32[2,2,3,180]{3,1,2,0:T(2,128)S(1)}, u32[]{:S(2)}, u32[]{:S(2)}) %collective-permute-start) | collective-permute-done | bytes 8672 | tf_op jit(solution)/shard_map/ppermute | solution.py:127
  43.9 8.3 %all-to-all-start = ((f32[2,2,3,96,128]{4,1,2,0,3:T(2,128)}), f32[2,2,3,96,128]{4,1,2,0,3:T(2,128)}, u32[]{:S(2)}, u32[]{:S(2)}) async-start(f32[2,2,3,96,128]{4,1,2,0,3:T(2,128)} %copy.388), calls=%async_computation | async-start | bytes 1179648 | tf_op jit(solution)/shard_map/all_to_all | solution.py:99
  55.1 8.9 %all-to-all-done = f32[2,2,3,96,128]{4,1,2,0,3:T(2,128)} async-done(((f32[2,2,3,96,128]{4,1,2,0,3:T(2,128)}), f32[2,2,3,96,128]{4,1,2,0,3:T(2,128)}, u32[]{:S(2)}, u32[]{:S(2)}) %all-to-all-start) | async-done | bytes 589856 | tf_op jit(solution)/shard_map/all_to_all | solution.py:99
  64.0 4.7 %all-to-all-start.2 = ((f32[2,2,3,96,128]{4,1,2,0,3:T(2,128)}), f32[2,2,3,96,128]{4,1,2,0,3:T(2,128)S(1)}, u32[]{:S(2)}, u32[]{:S(2)}) async-start(f32[2,2,3,96,128]{4,1,2,0,3:T(2,128)} %copy.402), calls=%async_computation.2 | async-start | bytes 1179648 | tf_op jit(solution)/shard_map/all_to_all | solution.py:99
  92.0 4.6 %all-to-all-start.1 = ((f32[2,2,96,3,128]{4,1,3,0,2:T(2,128)}), f32[2,2,96,3,128]{4,1,3,0,2:T(2,128)}, u32[]{:S(2)}, u32[]{:S(2)}) async-start(f32[2,2,96,3,128]{4,1,3,0,2:T(2,128)} %copy.396), calls=%async_computation.1 | async-start | bytes 1179648 | tf_op jit(solution)/shard_map/all_to_all | solution.py:105
  102.9 5.6 %all-to-all-done.1 = f32[2,2,96,3,128]{4,1,3,0,2:T(2,128)} async-done(((f32[2,2,96,3,128]{4,1,3,0,2:T(2,128)}), f32[2,2,96,3,128]{4,1,3,0,2:T(2,128)}, u32[]{:S(2)}, u32[]{:S(2)}) %all-to-all-start.1) | async-done | bytes 589856 | tf_op jit(solution)/shard_map/all_to_all | solution.py:105
  108.4 4.1 %all-to-all-start.3 = ((f32[2,2,96,3,128]{4,1,3,0,2:T(2,128)}), f32[2,2,96,3,128]{4,1,3,0,2:T(2,128)S(1)}, u32[]{:S(2)}, u32[]{:S(2)}) async-start(f32[2,2,96,3,128]{4,1,3,0,2:T(2,128)} %copy.410), calls=%async_computation.3 | async-start | bytes 1179648 | tf_op jit(solution)/shard_map/all_to_all | solution.py:105
  115.5 8.9 %all-to-all-done.3 = f32[2,2,96,3,128]{4,1,3,0,2:T(2,128)S(1)} async-done(((f32[2,2,96,3,128]{4,1,3,0,2:T(2,128)}), f32[2,2,96,3,128]{4,1,3,0,2:T(2,128)S(1)}, u32[]{:S(2)}, u32[]{:S(2)}) %all-to-all-start.3) | async-done | bytes 589856 | tf_op jit(solution)/shard_map/all_to_all | solution.py:105
  132.0 5.3 %all-to-all-start.4 = ((bf16[4,2,3,180,256]{4,1,3,2,0:T(2,128)(2,1)}), bf16[4,2,3,180,256]{4,1,3,2,0:T(2,128)(2,1)}, u32[]{:S(2)}, u32[]{:S(2)}) async-start(bf16[4,2,3,180,256]{4,1,3,2,0:T(2,128)(2,1)} %stack.121), calls=%async_computation.4 | async-start | bytes 4423680 | tf_op jit(solution)/shard_map/all_to_all | solution.py:260
  146.3 19.9 %all-to-all-done.4 = bf16[4,2,3,180,256]{4,1,3,2,0:T(2,128)(2,1)} async-done(((bf16[4,2,3,180,256]{4,1,3,2,0:T(2,128)(2,1)}), bf16[4,2,3,180,256]{4,1,3,2,0:T(2,128)(2,1)}, u32[]{:S(2)}, u32[]{:S(2)}) %all-to-all-start.4) | async-done | bytes 2211872 | tf_op jit(solution)/shard_map/all_to_all | solution.py:260
  166.1 5.4 %fusion.18 = (f32[2,3,180]{0,2,1:T(8,128)S(1)}, f32[2,3,180]{0,2,1:T(8,128)S(1)}) fusion(bf16[4,2,3,180,256]{4,1,3,2,0:T(2,128)(2,1)} %all-to-all-done.4), kind=kLoop, calls=%fused_computation.23 | loop fusion | flops 4421520 | bytes 2220480 | tf_op jit(solution)/shard_map/reduce_sum | solution.py:263
  178.8 6.9 %reshape.436 = f32[2,3,180,1024]{3,2,1,0:T(8,128)} reshape(f32[2,3,180,4,256]{4,3,2,1,0:T(4,128)} %copy.417) | data formatting | bytes 8847360 | tf_op jit(solution)/shard_map/convert_element_type | solution.py:262
  185.7 7.1 %fusion.7 = f32[2,3,180,1024]{3,2,1,0:T(8,128)} fusion(f32[2,3,180,1024]{3,2,1,0:T(8,128)} %reshape.436, f32[2,3,180]{2,1,0:T(4,128)S(1)} %get-tuple-element.60, f32[2,3,180]{2,1,0:T(4,128)S(1)} %get-tuple-element.59, bf16[1024,1024]{1,0:T(8,128)(2,1)S(1)} %copy-done), kind=kOutput, calls=%fused_computation.14 | convolution fusion | flops 2268241920 | bytes 10953152 | tf_op jit(solution)/shard_map/brwd,dh->brwh/dot_general | solution.py:267
  192.9 11.3 %fusion.546 = (f32[2,3,180]{2,1,0:T(4,128)S(1)}, f32[2,3,180]{2,1,0:T(4,128)S(1)}, bf16[2,3,180,1024]{3,2,1,0:T(8,128)(2,1)}) fusion(f32[2,3,180]{2,1,0:T(4,128)S(1)} %get-tuple-element.60, f32[2,3,180,1024]{3,2,1,0:T(8,128)} %reshape.436, f32[2,3,180]{2,1,0:T(4,128)S(1)} %get-tuple-element.59, bf16[1024,1024]{1,0:T(8,128)(2,1)S(1)} %copy-done, ...), kind=kOutput, calls=%fused_computation.645 | convolution fusion | flops 4547540992 | bytes 17482624 | tf_op jit(solution)/shard_map/brwh,dh->brwd/dot_general | solution.py:279
  205.8 6.2 %fusion.24 = bf16[2,3,180,1024]{3,2,1,0:T(8,128)(2,1)} fusion(bf16[1024,1024]{1,0:T(8,128)(2,1)S(1)} %copy-done.46, f32[2,3,180,1024]{3,2,1,0:T(8,128)} %fusion.7), kind=kOutput, calls=%fused_computation.33 | convolution fusion | flops 2271559680 | bytes 8732672 | tf_op jit(solution)/shard_map/brwh,hd->brwd/dot_general | solution.py:271
  216.7 5.1 %collective-permute-done.6 = f32[2,2,3,180]{3,1,2,0:T(2,128)S(1)} collective-permute-done((f32[2,2,3,180]{3,1,2,0:T(2,128)S(1)}, f32[2,2,3,180]{3,1,2,0:T(2,128)S(1)}, u32[]{:S(2)}, u32[]{:S(2)}) %collective-permute-start.6) | collective-permute-done | bytes 8672 | tf_op jit(solution)/shard_map/ppermute | solution.py:127
  221.8 9.6 %reduce-scatter.5.cloned.1.call-done = bf16[2,3,180,256]{3,2,1,0:T(8,128)(2,1)} async-done(((bf16[2,3,180,1024]{3,2,1,0:T(8,128)(2,1)}), bf16[2,3,180,256]{3,2,1,0:T(8,128)(2,1)}) %reduce-scatter.5.cloned.1.call-update) | async-done | bytes 552976 | tf_op jit(solution)/shard_map/reduce_scatter | solution.py:153
  231.4 33.4 %reduce-scatter.3.cloned.1.call-done = bf16[2,3,180,256]{3,2,1,0:T(8,128)(2,1)} async-done(((bf16[2,3,180,1024]{3,2,1,0:T(8,128)(2,1)}), bf16[2,3,180,256]{3,2,1,0:T(8,128)(2,1)}) %reduce-scatter.3.cloned.1.call-update) | async-done | bytes 552976 | tf_op jit(solution)/shard_map/reduce_scatter | solution.py:153
  269.6 7.4 %all-to-all-start.7 = ((f32[2,2,3,96,128]{4,1,2,0,3:T(2,128)}), f32[2,2,3,96,128]{4,1,2,0,3:T(2,128)S(1)}, u32[]{:S(2)}, u32[]{:S(2)}) async-start(f32[2,2,3,96,128]{4,1,2,0,3:T(2,128)} %copy.443), calls=%async_computation.9 | async-start | bytes 1179648 | tf_op jit(solution)/shard_map/all_to_all | solution.py:99
  279.2 9.6 %all-to-all-done.7 = f32[2,2,3,96,128]{4,1,2,0,3:T(2,128)S(1)} async-done(((f32[2,2,3,96,128]{4,1,2,0,3:T(2,128)}), f32[2,2,3,96,128]{4,1,2,0,3:T(2,128)S(1)}, u32[]{:S(2)}, u32[]{:S(2)}) %all-to-all-start.7) | async-done | bytes 589856 | tf_op jit(solution)/shard_map/all_to_all | solution.py:99
  294.8 9.9 %all-to-all-done.5 = f32[2,2,3,96,128]{4,1,2,0,3:T(2,128)S(1)} async-done(((f32[2,2,3,96,128]{4,1,2,0,3:T(2,128)}), f32[2,2,3,96,128]{4,1,2,0,3:T(2,128)S(1)}, u32[]{:S(2)}, u32[]{:S(2)}) %all-to-all-start.5) | async-done | bytes 589856 | tf_op jit(solution)/shard_map/all_to_all | solution.py:99
  315.2 5.0 %all-to-all-start.6 = ((f32[2,2,96,3,128]{4,1,3,0,2:T(2,128)}), f32[2,2,96,3,128]{4,1,3,0,2:T(2,128)}, u32[]{:S(2)}, u32[]{:S(2)}) async-start(f32[2,2,96,3,128]{4,1,3,0,2:T(2,128)} %copy.437), calls=%async_computation.8 | async-start | bytes 1179648 | tf_op jit(solution)/shard_map/all_to_all | solution.py:105
  332.0 7.0 %all-to-all-start.8 = ((f32[2,2,96,3,128]{4,1,3,0,2:T(2,128)}), f32[2,2,96,3,128]{4,1,3,0,2:T(2,128)S(1)}, u32[]{:S(2)}, u32[]{:S(2)}) async-start(f32[2,2,96,3,128]{4,1,3,0,2:T(2,128)} %copy.451), calls=%async_computation.10 | async-start | bytes 1179648 | tf_op jit(solution)/shard_map/all_to_all | solution.py:105
  341.3 9.5 %all-to-all-done.8 = f32[2,2,96,3,128]{4,1,3,0,2:T(2,128)S(1)} async-done(((f32[2,2,96,3,128]{4,1,3,0,2:T(2,128)}), f32[2,2,96,3,128]{4,1,3,0,2:T(2,128)S(1)}, u32[]{:S(2)}, u32[]{:S(2)}) %all-to-all-start.8) | async-done | bytes 589856 | tf_op jit(solution)/shard_map/all_to_all | solution.py:105
  (290 shorter events, 135.1 us)
Async XLA Ops:
  7.2 178.5 %copy-start = (bf16[1024,1024]{1,0:T(8,128)(2,1)S(1)}, bf16[1024,1024]{1,0:T(8,128)(2,1)}, u32[]{:S(2)}) copy-start(bf16[1024,1024]{1,0:T(8,128)(2,1)} %param.14) | copy-start | bytes 6291460
  7.2 94.3 %collective-permute-start.4 = (bf16[2,3,180,256]{3,0,2,1:T(2,128)(2,1)}, bf16[2,3,180,256]{3,0,2,1:T(2,128)(2,1)}, u32[]{:S(2)}, u32[]{:S(2)}) collective-permute-start(bf16[2,3,180,256]{3,0,2,1:T(2,128)(2,1)} %param.9), channel_id=1, source_target_pairs={{0,3},{1,0},{2,1},{3,2},{4,7},{5,4},{6,5},{7,6},{8,11},{9,8},{10,9... | collective-permute-start | bytes 1658888 | tf_op jit(solution)/shard_map/ppermute | solution.py:135
  10.3 91.2 %collective-permute-start.3 = (bf16[2,3,180,256]{3,0,2,1:T(2,128)(2,1)}, bf16[2,3,180,256]{3,0,2,1:T(2,128)(2,1)}, u32[]{:S(2)}, u32[]{:S(2)}) collective-permute-start(bf16[2,3,180,256]{3,0,2,1:T(2,128)(2,1)} %param.9), channel_id=1, source_target_pairs={{0,2},{1,3},{2,0},{3,1},{4,6},{5,7},{6,4},{7,5},{8,10},{9,11},{10,... | collective-permute-start | bytes 1658888 | tf_op jit(solution)/shard_map/ppermute | solution.py:135
  11.0 90.6 %collective-permute-start.2 = (bf16[2,3,180,256]{3,0,2,1:T(2,128)(2,1)}, bf16[2,3,180,256]{3,0,2,1:T(2,128)(2,1)}, u32[]{:S(2)}, u32[]{:S(2)}) collective-permute-start(bf16[2,3,180,256]{3,0,2,1:T(2,128)(2,1)} %param.9), channel_id=1, source_target_pairs={{0,1},{1,2},{2,3},{3,0},{4,5},{5,6},{6,7},{7,4},{8,9},{9,10},{10,1... | collective-permute-start | bytes 1658888 | tf_op jit(solution)/shard_map/ppermute | solution.py:135
  13.5 21.3 %collective-permute-start = (f32[2,2,3,180]{3,1,2,0:T(2,128)S(1)}, f32[2,2,3,180]{3,1,2,0:T(2,128)S(1)}, u32[]{:S(2)}, u32[]{:S(2)}) collective-permute-start(f32[2,2,3,180]{3,1,2,0:T(2,128)S(1)} %copy.384), channel_id=1, source_target_pairs={{0,1},{1,0},{2,3},{3,2},{4,5},{5,4},{6,7},{7,6},{8,9},{9,8},{10,11... | collective-permute-start | bytes 25928 | tf_op jit(solution)/shard_map/ppermute | solution.py:127
  34.9 5.3 %collective-permute-start.1 = (f32[2,2,3,180]{3,1,2,0:T(2,128)S(1)}, f32[2,2,3,180]{3,1,2,0:T(2,128)S(1)}, u32[]{:S(2)}, u32[]{:S(2)}) collective-permute-start(f32[2,2,3,180]{3,1,2,0:T(2,128)S(1)} %copy.386), channel_id=1, source_target_pairs={{0,2},{1,3},{2,0},{3,1},{4,6},{5,7},{6,4},{7,5},{8,10},{9,11},{10,... | collective-permute-start | bytes 25928 | tf_op jit(solution)/shard_map/ppermute | solution.py:127
  43.9 20.1 %all-to-all-start = ((f32[2,2,3,96,128]{4,1,2,0,3:T(2,128)}), f32[2,2,3,96,128]{4,1,2,0,3:T(2,128)}, u32[]{:S(2)}, u32[]{:S(2)}) async-start(f32[2,2,3,96,128]{4,1,2,0,3:T(2,128)} %copy.388), calls=%async_computation | async-start | bytes 1179648 | tf_op jit(solution)/shard_map/all_to_all | solution.py:99
  64.0 16.0 %all-to-all-start.2 = ((f32[2,2,3,96,128]{4,1,2,0,3:T(2,128)}), f32[2,2,3,96,128]{4,1,2,0,3:T(2,128)S(1)}, u32[]{:S(2)}, u32[]{:S(2)}) async-start(f32[2,2,3,96,128]{4,1,2,0,3:T(2,128)} %copy.402), calls=%async_computation.2 | async-start | bytes 1179648 | tf_op jit(solution)/shard_map/all_to_all | solution.py:99
  92.0 16.4 %all-to-all-start.1 = ((f32[2,2,96,3,128]{4,1,3,0,2:T(2,128)}), f32[2,2,96,3,128]{4,1,3,0,2:T(2,128)}, u32[]{:S(2)}, u32[]{:S(2)}) async-start(f32[2,2,96,3,128]{4,1,3,0,2:T(2,128)} %copy.396), calls=%async_computation.1 | async-start | bytes 1179648 | tf_op jit(solution)/shard_map/all_to_all | solution.py:105
  108.4 16.0 %all-to-all-start.3 = ((f32[2,2,96,3,128]{4,1,3,0,2:T(2,128)}), f32[2,2,96,3,128]{4,1,3,0,2:T(2,128)S(1)}, u32[]{:S(2)}, u32[]{:S(2)}) async-start(f32[2,2,96,3,128]{4,1,3,0,2:T(2,128)} %copy.410), calls=%async_computation.3 | async-start | bytes 1179648 | tf_op jit(solution)/shard_map/all_to_all | solution.py:105
  132.0 34.1 %all-to-all-start.4 = ((bf16[4,2,3,180,256]{4,1,3,2,0:T(2,128)(2,1)}), bf16[4,2,3,180,256]{4,1,3,2,0:T(2,128)(2,1)}, u32[]{:S(2)}, u32[]{:S(2)}) async-start(bf16[4,2,3,180,256]{4,1,3,2,0:T(2,128)(2,1)} %stack.121), calls=%async_computation.4 | async-start | bytes 4423680 | tf_op jit(solution)/shard_map/all_to_all | solution.py:260
  137.4 94.1 %reduce-scatter.5.cloned.1.call-start = ((), (), s32[]{:S(2)}) async-start(), calls=%async_computation.12 | async-start | bytes 2826240 | tf_op jit(solution)/shard_map/reduce_scatter | solution.py:153
  204.2 60.5 %reduce-scatter.3.cloned.1.call-start = ((), (), s32[]{:S(2)}) async-start(), calls=%async_computation.11 | async-start | bytes 2826240 | tf_op jit(solution)/shard_map/reduce_scatter | solution.py:153
  212.0 52.8 %copy-start.5 = (bf16[2,3,180,256]{3,2,1,0:T(8,128)(2,1)S(1)}, bf16[2,3,180,256]{3,2,1,0:T(8,128)(2,1)}, u32[]{:S(2)}) copy-start(bf16[2,3,180,256]{3,2,1,0:T(8,128)(2,1)} %copy-done.4) | copy-start | bytes 1658884
  212.0 52.8 %copy-start.35 = (bf16[2,3,180,256]{3,0,2,1:T(2,128)(2,1)S(1)}, bf16[2,3,180,256]{3,0,2,1:T(2,128)(2,1)}, u32[]{:S(2)}) copy-start(bf16[2,3,180,256]{3,0,2,1:T(2,128)(2,1)} %param.9) | copy-start | bytes 1658884
  212.0 55.3 %copy-start.32 = (f32[180,91]{1,0:T(8,128)S(1)}, f32[180,91]{1,0:T(8,128)}, u32[]{:S(2)}) copy-start(f32[180,91]{1,0:T(8,128)} %copy-done.31) | copy-start | bytes 196564
  212.0 4.0 %collective-permute-start.5 = (f32[2,2,3,180]{3,1,2,0:T(2,128)S(1)}, f32[2,2,3,180]{3,1,2,0:T(2,128)S(1)}, u32[]{:S(2)}, u32[]{:S(2)}) collective-permute-start(f32[2,2,3,180]{3,1,2,0:T(2,128)S(1)} %copy.425), channel_id=1, source_target_pairs={{0,1},{1,0},{2,3},{3,2},{4,5},{5,4},{6,7},{7,6},{8,9},{9,8},{10,11... | collective-permute-start | bytes 25928 | tf_op jit(solution)/shard_map/ppermute | solution.py:127
  216.1 5.7 %collective-permute-start.6 = (f32[2,2,3,180]{3,1,2,0:T(2,128)S(1)}, f32[2,2,3,180]{3,1,2,0:T(2,128)S(1)}, u32[]{:S(2)}, u32[]{:S(2)}) collective-permute-start(f32[2,2,3,180]{3,1,2,0:T(2,128)S(1)} %copy.427), channel_id=1, source_target_pairs={{0,2},{1,3},{2,0},{3,1},{4,6},{5,7},{6,4},{7,5},{8,10},{9,11},{10,... | collective-permute-start | bytes 25928 | tf_op jit(solution)/shard_map/ppermute | solution.py:127
  269.6 19.2 %all-to-all-start.7 = ((f32[2,2,3,96,128]{4,1,2,0,3:T(2,128)}), f32[2,2,3,96,128]{4,1,2,0,3:T(2,128)S(1)}, u32[]{:S(2)}, u32[]{:S(2)}) async-start(f32[2,2,3,96,128]{4,1,2,0,3:T(2,128)} %copy.443), calls=%async_computation.9 | async-start | bytes 1179648 | tf_op jit(solution)/shard_map/all_to_all | solution.py:99
  288.8 15.9 %all-to-all-start.5 = ((f32[2,2,3,96,128]{4,1,2,0,3:T(2,128)}), f32[2,2,3,96,128]{4,1,2,0,3:T(2,128)S(1)}, u32[]{:S(2)}, u32[]{:S(2)}) async-start(f32[2,2,3,96,128]{4,1,2,0,3:T(2,128)} %copy.429), calls=%async_computation.7 | async-start | bytes 1179648 | tf_op jit(solution)/shard_map/all_to_all | solution.py:99
  315.2 16.8 %all-to-all-start.6 = ((f32[2,2,96,3,128]{4,1,3,0,2:T(2,128)}), f32[2,2,96,3,128]{4,1,3,0,2:T(2,128)}, u32[]{:S(2)}, u32[]{:S(2)}) async-start(f32[2,2,96,3,128]{4,1,3,0,2:T(2,128)} %copy.437), calls=%async_computation.8 | async-start | bytes 1179648 | tf_op jit(solution)/shard_map/all_to_all | solution.py:105
  332.0 18.8 %all-to-all-start.8 = ((f32[2,2,96,3,128]{4,1,3,0,2:T(2,128)}), f32[2,2,96,3,128]{4,1,3,0,2:T(2,128)S(1)}, u32[]{:S(2)}, u32[]{:S(2)}) async-start(f32[2,2,96,3,128]{4,1,3,0,2:T(2,128)} %copy.451), calls=%async_computation.10 | async-start | bytes 1179648 | tf_op jit(solution)/shard_map/all_to_all | solution.py:105
  354.1 3.8 %collective-permute-start.7 = (f32[2,2,3,180]{3,1,2,0:T(2,128)S(1)}, f32[2,2,3,180]{3,1,2,0:T(2,128)S(1)}, u32[]{:S(2)}, u32[]{:S(2)}) collective-permute-start(f32[2,2,3,180]{3,1,2,0:T(2,128)S(1)} %copy.457), channel_id=1, source_target_pairs={{0,1},{1,0},{2,3},{3,2},{4,5},{5,4},{6,7},{7,6},{8,9},{9,8},{10,11... | collective-permute-start | bytes 25928 | tf_op jit(solution)/shard_map/ppermute | solution.py:127
  357.9 5.3 %collective-permute-start.8 = (f32[2,2,3,180]{3,1,2,0:T(2,128)S(1)}, f32[2,2,3,180]{3,1,2,0:T(2,128)S(1)}, u32[]{:S(2)}, u32[]{:S(2)}) collective-permute-start(f32[2,2,3,180]{3,1,2,0:T(2,128)S(1)} %copy.459), channel_id=1, source_target_pairs={{0,2},{1,3},{2,0},{3,1},{4,6},{5,7},{6,4},{7,5},{8,10},{9,11},{10,... | collective-permute-start | bytes 25928 | tf_op jit(solution)/shard_map/ppermute | solution.py:127
  (43 other events, 228.1 us)
Sparse Core Ops, SparseCore 0:
  204.3 27.0 reduce-scatter.4
  234.0 30.7 reduce-scatter.2
